TPU v7x, 512 devices: a whole 4x4x16 slice. The times are simulated.
512 devices in a mesh: grp: 4 (over y), seq: 32 (over z, core), mp: 4 (over x).
Axes of the slice: x: 4, y: 4, z: 16, core: 2. Of those that a mesh axis runs over, the one named last changes fastest.
Arguments:
- queries: bfloat16 [4, 4096, 2048], P('grp', 'seq', 'mp'), may hold values from -16 to 16
- d_out: bfloat16 [4, 4096, 2048], P('grp', 'seq', 'mp'), may hold values from -6 to 6
- neighbour_kv: bfloat16 [4, 256, 128, 2, 2048], P('grp', 'seq', None, None, 'mp'), may hold values from -16 to 16
- target: int32 [4, 256], P('grp', 'seq'), may hold values from -1 to 127, as said below
- bias: float32 [16, 191], P('mp'), may hold values from -6 to 6
Outputs:
- attended: bfloat16 [4, 4096, 2048], P('grp', 'seq', 'mp')
- d_query: bfloat16 [4, 4096, 2048], P('grp', 'seq', 'mp')
- d_kv: bfloat16 [4, 256, 128, 2, 2048], P('grp', 'seq', None, None, 'mp')
- d_bias: float32 [16, 191], P('mp')
Inputs may be any that keep to these rules, and one draw needn't show every extreme that they name: `target`: in each group every entry 0..127 stands in exactly one slot and -1 marks an empty slot. The slots of one index of seq hold at most 1 entries e with the same e // 4, and some index reaches that; some index of seq holds 8 entries.
All inputs are finite; a program needn't handle non-finite values.
Results may differ from a plain program's by a relative error of at most 0.011.
Values may be sent and summed in bfloat16 or wider, within the bound.
No kernel may reach another device: no remote copies, remote signals or barrier semaphores. Data moves between devices by JAX's collectives and lax.ppermute only.
A program may use at most 128 MiB of HBM per device.

v0:
```python
import jax
import jax.numpy as jnp
from jax import lax
from jax.sharding import PartitionSpec as P

STRETCH = 64
NB_LEN = 128
SEQ_LEN = 2048


def passed_along(block, axis, distance):
    devices = range(lax.axis_size(axis))
    route = [(i - distance, i) for i in devices if i - distance in devices]
    return lax.ppermute(block, axis, route)


def bias_grid(lookup, row_count, col_count):
    head_num = lookup.shape[0]
    span = row_count + col_count
    padded = jnp.pad(lookup, ((0, 0), (0, 1)))
    flattened = jnp.tile(padded, (1, row_count))
    flattened = jnp.pad(flattened, ((0, 0), (0, row_count)))
    shaped = flattened.reshape(head_num, row_count, span + 1)[:, :, :col_count]
    return shaped[:, :, ::-1]


def bias_fold(grads):
    head_num, row_count, col_count = grads.shape
    turned = grads[:, :, ::-1]
    padded = jnp.pad(turned, ((0, 0), (0, 0), (0, row_count)))
    flattened = padded.reshape(head_num, row_count * (row_count + col_count))
    flattened = flattened[:, : row_count * (row_count + col_count - 1)]
    return jnp.sum(flattened.reshape(head_num, row_count, row_count + col_count - 1), axis=1)


def take_rows(table, index, valid):
    rows = jnp.take(table, index, axis=0)
    shape = (valid.shape[0],) + (1,) * (rows.ndim - 1)
    return jnp.where(valid.reshape(shape), rows, jnp.zeros((), rows.dtype))


def exchange(block):
    return lax.all_to_all(block, "seq", split_axis=0, concat_axis=0, tiled=True)


def local(queries, d_out, neighbour_kv, target, bias):
    tok_rows = queries.shape[1]
    width_dev = queries.shape[2]
    head_count = bias.shape[0]
    head_depth = width_dev // head_count
    stretch_count = tok_rows // STRETCH
    per_owner = 2 * stretch_count
    shard_count = lax.axis_size("seq")
    my_index = lax.axis_index("seq")
    group_rows = tok_rows * shard_count
    seq_stretches = min(SEQ_LEN, group_rows) // STRETCH
    scale_factor = head_depth ** (-0.5)
    bias_rows = bias_grid(bias, STRETCH, NB_LEN).transpose(1, 0, 2)
    row_ids = jnp.arange(STRETCH)
    pair = jnp.stack([queries[0], d_out[0]], axis=1)
    pair_all = lax.all_gather(pair, "seq", axis=0, tiled=True)
    my_targets = target[0]
    slot_count = my_targets.shape[0]
    is_used = my_targets >= 0
    entry = jnp.where(is_used, my_targets, 0)
    stretch_of = entry // 2
    win_rows = stretch_of[:, None] * STRETCH + (STRETCH - 1) + row_ids[None, :]
    in_group = win_rows < group_rows
    win_rows = jnp.minimum(win_rows.reshape(-1), group_rows - 1)
    win = jnp.take(pair_all, win_rows, axis=0).reshape(slot_count, STRETCH, 2, width_dev)
    q_win = win[:, :, 0]
    g_win = win[:, :, 1]
    live_slot = (row_ids[None, :] == 0) | ((stretch_of[:, None] + 1) % seq_stretches != 0)
    q_keep = is_used[:, None] & in_group
    q_slots = jnp.where(q_keep[:, :, None], q_win, jnp.zeros((), q_win.dtype))
    g_slots = jnp.where((q_keep & live_slot)[:, :, None], g_win, jnp.zeros((), g_win.dtype))
    q_slots = q_slots.reshape(slot_count, STRETCH, head_count, head_depth)
    g_slots = g_slots.reshape(slot_count, STRETCH, head_count, head_depth)
    stored = neighbour_kv[0]
    key_rows = stored[:, :, 0].reshape(slot_count, NB_LEN, head_count, head_depth)
    value_rows = stored[:, :, 1].reshape(slot_count, NB_LEN, head_count, head_depth)
    scores = jnp.einsum("sihd,sjhd->sihj", q_slots, key_rows, preferred_element_type=jnp.float32)
    scores = scores * scale_factor + bias_rows[None]
    peak_val = jnp.max(scores, axis=-1)
    weights = jnp.exp(scores - peak_val[..., None])
    row_total = jnp.sum(weights, axis=-1)
    partial_value = jnp.einsum(
        "sihj,sjhd->sihd",
        weights.astype(jnp.bfloat16),
        value_rows,
        preferred_element_type=jnp.float32,
    )
    owner_of = jnp.where(is_used, my_targets // per_owner, -1)
    owner_match = owner_of[None, :] == jnp.arange(shard_count)[:, None]
    send_slot = jnp.argmax(owner_match, axis=1)
    send_has = jnp.any(owner_match, axis=1)
    part_send = take_rows(
        partial_value.astype(jnp.bfloat16).reshape(slot_count, STRETCH, width_dev),
        send_slot,
        send_has,
    )
    g_dot = jnp.einsum(
        "sihd,sihd->sih",
        g_slots.astype(jnp.float32),
        partial_value,
        precision=lax.Precision.HIGHEST,
    )
    mine = jnp.stack([peak_val, row_total, g_dot], axis=1)
    shared = jnp.concatenate(
        [
            mine.reshape(slot_count, -1),
            jnp.where(is_used, entry + 1, 0).astype(jnp.float32)[:, None],
        ],
        axis=1,
    )
    shared_wide = jnp.pad(shared, ((0, 0), (0, 1024 - shared.shape[1])))
    shared_all = lax.all_gather(shared_wide, "seq", tiled=True)[:, : shared.shape[1]]
    partner = entry + 1 - 2 * (entry % 2)
    partner_at = jnp.argmax(
        shared_all[None, :, -1] == (partner + 1).astype(jnp.float32)[:, None], axis=1
    )
    theirs = jnp.take(shared_all[:, :-1], partner_at, axis=0).reshape(mine.shape)
    both_peak = jnp.maximum(mine[:, 0], theirs[:, 0])
    mine_f = jnp.exp(mine[:, 0] - both_peak)
    theirs_f = jnp.exp(theirs[:, 0] - both_peak)
    both_total = mine_f * mine[:, 1] + theirs_f * theirs[:, 1]
    lse_slots = both_peak + jnp.log(both_total)
    dd_slots = (mine_f * mine[:, 2] + theirs_f * theirs[:, 2]) / both_total
    dd_slots = jnp.where(is_used[:, None, None], dd_slots, 0.0)
    part_recv = exchange(part_send)
    own_entries = my_index * per_owner + jnp.arange(per_owner)
    own_at = jnp.argmax(
        shared_all[None, :, -1] == (own_entries + 1).astype(jnp.float32)[:, None], axis=1
    )
    held_by = own_at // slot_count
    parts_own = jnp.take(part_recv, held_by, axis=0).astype(jnp.float32)
    parts_own = parts_own.reshape(stretch_count, 2, STRETCH, head_count, head_depth)
    stats_own = jnp.take(shared_all[:, :-1], own_at, axis=0).reshape(
        stretch_count, 2, 3, STRETCH, head_count
    )
    peaks_own = stats_own[:, :, 0]
    totals_own = stats_own[:, :, 1]
    stretch_ids = my_index * stretch_count + jnp.arange(stretch_count)
    is_live = (row_ids[None, :] == 0) | ((stretch_ids[:, None] + 1) % seq_stretches != 0)
    live_rows = is_live.astype(jnp.float32)
    top_peak = jnp.max(peaks_own, axis=1)
    factor = jnp.exp(peaks_own - top_peak[:, None])
    denominator = jnp.sum(factor * totals_own, axis=1)
    combined = jnp.sum(factor[..., None] * parts_own, axis=1) / denominator[..., None]
    combined = combined * live_rows[:, :, None, None]
    att_win = combined.astype(jnp.bfloat16).reshape(tok_rows, width_dev)
    att_before = passed_along(att_win[tok_rows - STRETCH :], "seq", 1)
    prob_full = jnp.exp(scores - lse_slots[..., None])
    prob_low = prob_full.astype(jnp.bfloat16)
    grad_prob = jnp.einsum(
        "sihd,sjhd->sihj", g_slots, value_rows, preferred_element_type=jnp.float32
    )
    grad_scores = prob_full * (grad_prob - dd_slots[..., None])
    scores_low = grad_scores.astype(jnp.bfloat16)
    grad_rows = (
        jnp.einsum("sihj,sjhd->sihd", scores_low, key_rows, preferred_element_type=jnp.float32)
        * scale_factor
    )
    mix_probs = jnp.stack([scores_low, prob_low], axis=1)
    mix_rows = jnp.stack([q_slots, g_slots], axis=1)
    grad_kv = jnp.einsum(
        "sxihj,sxihd->sjxhd", mix_probs, mix_rows, preferred_element_type=jnp.float32
    )
    kv_scale = jnp.array([scale_factor, 1.0], jnp.float32)[None, None, :, None, None]
    d_kv = (grad_kv * kv_scale).astype(jnp.bfloat16).reshape(slot_count, NB_LEN, 2, width_dev)
    bias_part = bias_fold(jnp.sum(grad_scores, axis=0).transpose(1, 0, 2))
    dq_rows = jnp.zeros((shard_count, stretch_count, STRETCH, width_dev), jnp.bfloat16)
    dq_owner = jnp.where(is_used, owner_of, shard_count)
    dq_rows = dq_rows.at[dq_owner, stretch_of % stretch_count].set(
        grad_rows.astype(jnp.bfloat16).reshape(slot_count, STRETCH, width_dev), mode="drop"
    )
    grad_win = lax.psum_scatter(dq_rows, "seq", scatter_dimension=0, tiled=True)
    grad_win = grad_win.reshape(tok_rows, width_dev)
    grad_before = passed_along(grad_win[tok_rows - STRETCH :], "seq", 1)
    attended = jnp.concatenate([att_before[1:], att_win[: tok_rows - STRETCH + 1]])
    d_query = jnp.concatenate([grad_before[1:], grad_win[: tok_rows - STRETCH + 1]])
    raw_sum = lax.psum(lax.psum(bias_part, "seq"), "grp")
    squares = lax.psum(jnp.sum(raw_sum * raw_sum), "mp")
    d_bias = raw_sum * jnp.minimum(1.0, 1.0 / jnp.sqrt(squares + 1e-12))
    return (attended[None], d_query[None], d_kv[None], d_bias)


def solution(mesh):
    in_specs = (
        P("grp", "seq", "mp"),
        P("grp", "seq", "mp"),
        P("grp", "seq", None, None, "mp"),
        P("grp", "seq"),
        P("mp", None),
    )
    out_specs = (
        P("grp", "seq", "mp"),
        P("grp", "seq", "mp"),
        P("grp", "seq", None, None, "mp"),
        P("mp", None),
    )
    return jax.shard_map(local, mesh=mesh, in_specs=in_specs, out_specs=out_specs, check_vma=False)
```

profile of v0, /device:TPU:1, one launch (start us, length us, event | category | flops | bytes accessed | tf_op | source)
XLA Modules:
  0.0 341.9 jit_solution(12824938684409181369)
XLA Ops:
  7.2 1.1 pad_maximum_fusion.1
  8.4 1.0 copy.104
  10.3 0.7 copy.111
  11.0 0.7 pad.16
  12.3 3.8 %copy.106 = bf16[1,8,128,2,512]{2,4,1,3,0:T(8,128)(2,1)} copy(bf16[1,8,128,2,512]{4,3,2,1,0:T(2,128)(2,1)S(1)} %copy-done.8) | data formatting | bytes 4194304 | tf_op args[2]
  16.9 2.8 fusion.54
  19.7 75.7 %all-gather.3.cloned.1.call-done = bf16[4096,2,512]{2,1,0:T(2,128)(2,1)} async-done(((bf16[128,2,512]{2,1,0:T(2,128)(2,1)}), bf16[4096,2,512]{2,1,0:T(2,128)(2,1)}) %all-gather.3.cloned.1.call-update) | async-done | bytes 8388624 | tf_op jit(solution)/shard_map/all_gather | solution.py:61
  95.4 6.4 %gather_fusion = bf16[512,2,512]{2,1,0:T(2,128)(2,1)S(1)} fusion(bf16[4096,2,512]{2,1,0:T(2,128)(2,1)} %all-gather.3.cloned.1.call-done, s32[1024]{0:T(1024)S(1)} %pad_clamp_fusion.4), kind=kCustom, calls=%fused_computation | custom fusion | bytes 2099200 | tf_op jit(solution)/shard_map/jit(_take)/gather | solution.py:70
  102.4 0.7 broadcast_select_fusion.1
  103.1 1.4 fusion.53
  105.1 2.0 multiply_reduce_fusion
  108.9 1.1 copy.160
  110.1 2.0 gather_fusion.2
  112.1 3.3 select_select_fusion
  115.3 7.8 %all-to-all-start = ((bf16[32,64,512]{2,1,0:T(8,128)(2,1)}), bf16[32,64,512]{2,1,0:T(8,128)(2,1)}, u32[]{:S(2)}, u32[]{:S(2)}) async-start(bf16[32,64,512]{2,1,0:T(8,128)(2,1)} %select_select_fusion), calls=%async_computation | async-start | bytes 4194304 | tf_op jit(solution)/shard_map/all_to_all | solution.py:43
  123.2 76.4 %all-gather.5.cloned.1.call-done = f32[256,1024]{1,0:T(8,128)} async-done(((f32[8,1024]{1,0:T(8,128)}), f32[256,1024]{1,0:T(8,128)}) %all-gather.5.cloned.1.call-update) | async-done | bytes 1048592 | tf_op jit(solution)/shard_map/all_gather | solution.py:117
  199.6 1.0 slice_reduce_fusion
  200.6 0.7 iota_reduce_fusion
  201.9 2.1 slice.108
  203.9 2.3 gather_fusion.4
  206.2 0.9 copy.120
  207.2 0.8 copy.121
  207.9 1.0 broadcast_select_fusion.3
  208.9 0.8 log_add_fusion
  209.7 0.8 fusion.3
  210.5 1.0 copy-done
  211.5 0.8 fusion.5
  212.4 2.4 broadcast_in_dim.169
  214.9 2.5 scatter_fusion
  218.4 0.9 squeeze.45
  219.3 1.0 squeeze.44
  220.3 1.0 fusion.55
  222.0 45.5 %psum.21 = f32[4,191]{1,0:T(4,128)S(1)} all-reduce(f32[4,191]{1,0:T(4,128)S(1)} %reduce_sum.58), channel_id=1, replica_groups=mesh['grp'=4,'seq'=32,'mp'=4] {'seq'}, use_global_device_ids=true, to_apply=%region_13.14 | all-reduce | flops 764 | bytes 6112 | tf_op jit(solution)/shard_map/psum | solution.py:182
  267.5 8.4 %psum.22 = f32[4,191]{1,0:T(4,128)S(1)} all-reduce(f32[4,191]{1,0:T(4,128)S(1)} %psum.21), channel_id=1, replica_groups=mesh['grp'=4,'seq'=32,'mp'=4] {'grp'}, use_global_device_ids=true, to_apply=%region_14.15 | all-reduce | flops 764 | bytes 6112 | tf_op jit(solution)/shard_map/psum | solution.py:182
  276.5 1.2 copy_select_fusion.1
  277.7 10.2 %psum.23 = f32[]{:T(128)} all-reduce(f32[]{:T(128)} %multiply_reduce_fusion.2), channel_id=1, replica_groups=mesh['grp'=4,'seq'=32,'mp'=4] {'mp'}, use_global_device_ids=true, to_apply=%region_16.17 | all-reduce | flops 1 | bytes 8 | tf_op jit(solution)/shard_map/psum | solution.py:183
  287.9 0.7 iota_reduce_fusion.2
  289.9 1.7 gather_fusion.1
  293.0 2.2 multiply_convert_fusion
  295.2 3.8 %copy.129 = bf16[1,8,128,2,512]{4,3,2,1,0:T(2,128)(2,1)} copy(bf16[1,8,128,2,512]{2,4,3,1,0:T(8,128)(2,1)S(1)} %bitcast.165) | data formatting | bytes 4194304
  299.8 2.2 gather_fusion.3
  302.9 5.1 %collective-permute-start = (bf16[64,512]{1,0:T(8,128)(2,1)S(1)}, bf16[64,512]{1,0:T(8,128)(2,1)S(1)}, u32[]{:S(2)}, u32[]{:S(2)}) collective-permute-start(bf16[64,512]{1,0:T(8,128)(2,1)S(1)} %bitcast.180), channel_id=1, source_target_pairs={{0,4},{4,8},{8,12},{12,16},{16,20},{20,24},{24,28},{28,32},{32,36}... | collective-permute-start | bytes 196616 | tf_op jit(solution)/shard_map/ppermute | solution.py:14
  308.2 1.9 collective-permute-done
  310.1 18.2 %reduce-scatter.2.cloned.1.call-done = bf16[1,2,64,512]{3,2,1,0:T(8,128)(2,1)} async-done(((bf16[32,2,64,512]{3,2,1,0:T(8,128)(2,1)}), bf16[1,2,64,512]{3,2,1,0:T(8,128)(2,1)}) %reduce-scatter.2.cloned.1.call-update) | async-done | bytes 131088 | tf_op jit(solution)/shard_map/reduce_scatter | solution.py:177
  328.3 0.8 slice_bitcast_fusion.1
  329.1 3.4 collective-permute-start.1
  332.6 0.7 maximum_bitcast_fusion
  333.2 0.9 slice.121
  (133 shorter events, 13.0 us)
Async XLA Ops:
  7.2 5.2 %copy-start.8 = (bf16[1,8,128,2,512]{4,3,2,1,0:T(2,128)(2,1)S(1)}, bf16[1,8,128,2,512]{4,3,2,1,0:T(2,128)(2,1)}, u32[]{:S(2)}) copy-start(bf16[1,8,128,2,512]{4,3,2,1,0:T(2,128)(2,1)} %param.8) | copy-start | bytes 6291460
  7.2 88.3 %all-gather.3.cloned.1.call-start = ((), (), s32[]{:S(2)}) async-start(), calls=%async_computation.2 | async-start | bytes 8650752 | tf_op jit(solution)/shard_map/all_gather | solution.py:61
  9.4 190.3 %all-gather.5.cloned.1.call-start = ((), (), s32[]{:S(2)}) async-start(), calls=%async_computation.3 | async-start | bytes 1081344 | tf_op jit(solution)/shard_map/all_gather | solution.py:117
  10.1 6.1 %copy-start.21 = (pred[8]{0:T(512)(128)(4,1)}, pred[8]{0:T(512)(128)(4,1)S(1)}, u32[]{:S(2)}) copy-start(pred[8]{0:T(512)(128)(4,1)S(1)} %get-tuple-element.54) | copy-start | bytes 28
  16.1 3.6 %copy-start.23 = (pred[64]{0:T(512)(128)(4,1)}, pred[64]{0:T(512)(128)(4,1)S(1)}, u32[]{:S(2)}) copy-start(pred[64]{0:T(512)(128)(4,1)S(1)} %iota_compare_fusion.2) | copy-start | bytes 196
  16.2 86.1 %copy-start.17 = (pred[8,64]{1,0:T(8,128)(4,1)}, pred[8,64]{1,0:T(8,128)(4,1)S(1)}, u32[]{:S(2)}) copy-start(pred[8,64]{1,0:T(8,128)(4,1)S(1)} %get-tuple-element.51) | copy-start | bytes 1540
  16.2 86.9 %copy-start.15 = (pred[8,64]{1,0:T(8,128)(4,1)}, pred[8,64]{1,0:T(8,128)(4,1)S(1)}, u32[]{:S(2)}) copy-start(pred[8,64]{1,0:T(8,128)(4,1)S(1)} %get-tuple-element.50) | copy-start | bytes 1540
  102.1 2.5 copy-start.4
  102.4 2.2 copy-start.2
  105.1 3.1 copy-start.22
  107.1 1.8 copy-start.12
  107.1 1.8 copy-start.13
  115.3 184.5 %all-to-all-start = ((bf16[32,64,512]{2,1,0:T(8,128)(2,1)}), bf16[32,64,512]{2,1,0:T(8,128)(2,1)}, u32[]{:S(2)}, u32[]{:S(2)}) async-start(bf16[32,64,512]{2,1,0:T(8,128)(2,1)} %select_select_fusion), calls=%async_computation | async-start | bytes 4194304 | tf_op jit(solution)/shard_map/all_to_all | solution.py:43
  123.2 86.5 %copy-start.9 = (bf16[8,64,4,128]{3,2,1,0:T(4,128)(2,1)S(1)}, bf16[8,64,4,128]{3,2,1,0:T(4,128)(2,1)}, u32[]{:S(2)}) copy-start(bf16[8,64,4,128]{3,2,1,0:T(4,128)(2,1)} %get-tuple-element.35) | copy-start | bytes 1572868
  123.2 205.1 %reduce-scatter.2.cloned.1.call-start = ((), (), s32[]{:S(2)}) async-start(), calls=%async_computation.4 | async-start | bytes 4325376 | tf_op jit(solution)/shard_map/reduce_scatter | solution.py:177
  200.6 3.3 copy-start.19
  207.9 3.5 %copy-start.3 = (bf16[8,128,1,512]{1,3,0,2:T(8,128)(2,1)S(1)}, bf16[8,128,1,512]{1,3,0,2:T(8,128)(2,1)}, u32[]{:S(2)}) copy-start(bf16[8,128,1,512]{1,3,0,2:T(8,128)(2,1)} %get-tuple-element.38) | copy-start | bytes 3145732
  209.7 2.6 copy-start.10
  210.5 1.0 copy-start
  212.4 2.4 copy-start.14
  217.4 0.7 copy-start.24
  217.4 1.0 copy-start.5
  217.4 3.0 copy-start.1
  219.3 57.2 %copy-start.6 = (bf16[8,1,64,4,128]{4,3,2,0,1:T(4,128)(2,1)S(1)}, bf16[8,1,64,4,128]{4,3,2,0,1:T(4,128)(2,1)}, u32[]{:S(2)}) copy-start(bf16[8,1,64,4,128]{4,3,2,0,1:T(4,128)(2,1)} %squeeze.45) | copy-start | bytes 1572868
  219.3 57.2 %copy-start.16 = (pred[8,64]{1,0:T(8,128)(4,1)S(1)}, pred[8,64]{1,0:T(8,128)(4,1)}, u32[]{:S(2)}) copy-start(pred[8,64]{1,0:T(8,128)(4,1)} %copy-done.15) | copy-start | bytes 1540
  219.3 57.2 %copy-start.18 = (pred[8,64]{1,0:T(8,128)(4,1)S(1)}, pred[8,64]{1,0:T(8,128)(4,1)}, u32[]{:S(2)}) copy-start(pred[8,64]{1,0:T(8,128)(4,1)} %copy-done.17) | copy-start | bytes 1540
  220.3 56.2 %copy-start.7 = (bf16[8,1,64,4,128]{4,3,2,0,1:T(4,128)(2,1)S(1)}, bf16[8,1,64,4,128]{4,3,2,0,1:T(4,128)(2,1)}, u32[]{:S(2)}) copy-start(bf16[8,1,64,4,128]{4,3,2,0,1:T(4,128)(2,1)} %squeeze.44) | copy-start | bytes 1572868
  221.3 66.6 %copy-start.20 = (f32[256]{0:T(256)S(1)}, f32[256]{0:T(256)}, u32[]{:S(2)}) copy-start(f32[256]{0:T(256)} %copy-done.19) | copy-start | bytes 3076
  221.4 71.2 %copy-start.11 = (f32[8,64,4]{1,2,0:T(4,128)S(1)}, f32[8,64,4]{1,2,0:T(4,128)}, u32[]{:S(2)}) copy-start(f32[8,64,4]{1,2,0:T(4,128)} %copy-done.10) | copy-start | bytes 24580
  295.2 3.8 %copy-start.26 = (pred[2,2]{1,0:T(4,128)(4,1)S(1)}, pred[2,2]{1,0:T(4,128)(4,1)}, u32[]{:S(2)}) copy-start(pred[2,2]{1,0:T(4,128)(4,1)} %broadcast_in_dim.155) | copy-start | bytes 16
  299.0 3.0 copy-start.25
  302.9 7.1 %collective-permute-start = (bf16[64,512]{1,0:T(8,128)(2,1)S(1)}, bf16[64,512]{1,0:T(8,128)(2,1)S(1)}, u32[]{:S(2)}, u32[]{:S(2)}) collective-permute-start(bf16[64,512]{1,0:T(8,128)(2,1)S(1)} %bitcast.180), channel_id=1, source_target_pairs={{0,4},{4,8},{8,12},{12,16},{16,20},{20,24},{24,28},{28,32},{32,36}... | collective-permute-start | bytes 196616 | tf_op jit(solution)/shard_map/ppermute | solution.py:14
  329.1 5.5 %collective-permute-start.1 = (bf16[64,512]{1,0:T(8,128)(2,1)S(1)}, bf16[64,512]{1,0:T(8,128)(2,1)S(1)}, u32[]{:S(2)}, u32[]{:S(2)}) collective-permute-start(bf16[64,512]{1,0:T(8,128)(2,1)S(1)} %slice_bitcast_fusion.1), channel_id=1, source_target_pairs={{0,4},{4,8},{8,12},{12,16},{16,20},{20,24},{24,28},{28,32},{32,36}... | collective-permute-start | bytes 196616 | tf_op jit(solution)/shard_map/ppermute | solution.py:14
Sparse Core Ops, SparseCore 0:
  10.1 85.2 all-gather.2
  108.3 91.2 all-gather.4
  217.5 110.7 reduce-scatter.1
where the time goes:
time: 343 us; the launch traced here: 342 us
  waiting for transfers between devices  173 us (50%)
  blocking collectives  64.2 us (19%)
  local copies, waits for them, and re-layouts  47.5 us (14%)
  other arithmetic  19.6 us (6%)
  starting transfers between devices  16.5 us (5%)
  between operations  15 us (4%)
  matrix products  6.32 us (2%)
    all_gather x1, waiting for transfers between devices, local(): lax.all_gather(shared_wide, 'seq', tiled=True)[:, :shared.shape[1]]  76.4 us
    all_gather x1, waiting for transfers between devices, local(): pair_all = lax.all_gather(pair, 'seq', axis=0, tiled=True)  75.7 us
    psum x2, blocking collectives, local(): raw_sum = lax.psum(lax.psum(bias_part, 'seq'), 'grp')  53.9 us
    reduce_scatter x1, waiting for transfers between devices, local(): grad_win = lax.psum_scatter(dq_rows, 'seq', scatter_dimension=0, tiled=True)  18.2 us
    psum x1, blocking collectives, local(): squares = lax.psum(jnp.sum(raw_sum * raw_sum), 'mp')  10.2 us
    unnamed x58, local copies, waits for them, and re-layouts  9.33 us
    ppermute x2, starting transfers between devices, passed_along(): return lax.ppermute(block, axis, route)  8.55 us
    all_to_all x1, starting transfers between devices, exchange(): return lax.all_to_all(block, 'seq', split_axis=0, concat_axis=0, tiled=True)  7.84 us
  transfers between devices with their start and end apart: 6, of which 5 were waited for; matrix products, arithmetic and copies ran while one was open for 16% of the time, Pallas kernels for 0%

commit v1 on v0

--- a/solution.py
+++ b/solution.py
@@ -179,7 +179,9 @@
     grad_before = passed_along(grad_win[tok_rows - STRETCH :], "seq", 1)
     attended = jnp.concatenate([att_before[1:], att_win[: tok_rows - STRETCH + 1]])
     d_query = jnp.concatenate([grad_before[1:], grad_win[: tok_rows - STRETCH + 1]])
-    raw_sum = lax.psum(lax.psum(bias_part, "seq"), "grp")
+    own = lax.psum(bias_part, "seq")
+    parts = lax.all_gather(own, "grp", axis=0, tiled=False)
+    raw_sum = parts.sum(axis=0)
     squares = lax.psum(jnp.sum(raw_sum * raw_sum), "mp")
     d_bias = raw_sum * jnp.minimum(1.0, 1.0 / jnp.sqrt(squares + 1e-12))
     return (attended[None], d_query[None], d_kv[None], d_bias)

time: 343 us -> 342 us (level)
    all_gather x0 -> x1, blocking collectives: none -> 9.6 us  [local(): parts = lax.all_gather(own, 'grp', axis=0, tiled=False)]
    psum x2 -> x1, blocking collectives: 53.9 us -> 46.7 us  [local(): own = lax.psum(bias_part, 'seq')]
    unnamed x58 -> x62, local copies, waits for them, and re-layouts: 9.33 us -> 9.33 us
where the time goes in v1:
time: 342 us; the launch traced here: 341 us
  waiting for transfers between devices  171 us (50%)
  blocking collectives  63.9 us (19%)
  local copies, waits for them, and re-layouts  47.5 us (14%)
  other arithmetic  19.7 us (6%)
  starting transfers between devices  17.9 us (5%)
  between operations  15 us (4%)
  matrix products  6 us (2%)
    all_gather x1, waiting for transfers between devices, local(): lax.all_gather(shared_wide, 'seq', tiled=True)[:, :shared.shape[1]]  78.4 us
    all_gather x1, waiting for transfers between devices, local(): pair_all = lax.all_gather(pair, 'seq', axis=0, tiled=True)  75.7 us
    psum x1, blocking collectives, local(): own = lax.psum(bias_part, 'seq')  46.7 us
    reduce_scatter x1, waiting for transfers between devices, local(): grad_win = lax.psum_scatter(dq_rows, 'seq', scatter_dimension=0, tiled=True)  14.9 us
    ppermute x2, starting transfers between devices, passed_along(): return lax.ppermute(block, axis, route)  9.98 us
    all_gather x1, blocking collectives, local(): parts = lax.all_gather(own, 'grp', axis=0, tiled=False)  9.6 us
    unnamed x62, local copies, waits for them, and re-layouts  9.33 us
    all_to_all x1, starting transfers between devices, exchange(): return lax.all_to_all(block, 'seq', split_axis=0, concat_axis=0, tiled=True)  7.84 us
  transfers between devices with their start and end apart: 6, of which 5 were waited for; matrix products, arithmetic and copies ran while one was open for 16% of the time, Pallas kernels for 0%

profile of v1, /device:TPU:1, one launch (start us, length us, event | category | flops | bytes accessed | tf_op | source)
XLA Modules:
  0.0 341.4 jit_solution(5611892943813630152)
XLA Ops:
  7.2 1.1 pad_maximum_fusion.1
  8.4 1.0 copy.104
  10.3 0.7 copy.111
  11.0 0.7 pad.16
  12.3 3.8 %copy.106 = bf16[1,8,128,2,512]{2,4,1,3,0:T(8,128)(2,1)} copy(bf16[1,8,128,2,512]{4,3,2,1,0:T(2,128)(2,1)S(1)} %copy-done.8) | data formatting | bytes 4194304 | tf_op args[2]
  16.9 2.8 fusion.54
  19.7 75.7 %all-gather.3.cloned.1.call-done = bf16[4096,2,512]{2,1,0:T(2,128)(2,1)} async-done(((bf16[128,2,512]{2,1,0:T(2,128)(2,1)}), bf16[4096,2,512]{2,1,0:T(2,128)(2,1)}) %all-gather.3.cloned.1.call-update) | async-done | bytes 8388624 | tf_op jit(solution)/shard_map/all_gather | solution.py:61
  95.4 6.4 %gather_fusion = bf16[512,2,512]{2,1,0:T(2,128)(2,1)S(1)} fusion(bf16[4096,2,512]{2,1,0:T(2,128)(2,1)} %all-gather.3.cloned.1.call-done, s32[1024]{0:T(1024)S(1)} %pad_clamp_fusion.4), kind=kCustom, calls=%fused_computation | custom fusion | bytes 2099200 | tf_op jit(solution)/shard_map/jit(_take)/gather | solution.py:70
  102.4 0.7 broadcast_select_fusion.1
  103.1 1.4 fusion.53
  105.1 2.0 multiply_reduce_fusion
  108.9 1.1 copy.160
  110.1 2.0 gather_fusion.2
  112.1 3.3 select_select_fusion
  115.3 7.8 %all-to-all-start = ((bf16[32,64,512]{2,1,0:T(8,128)(2,1)}), bf16[32,64,512]{2,1,0:T(8,128)(2,1)}, u32[]{:S(2)}, u32[]{:S(2)}) async-start(bf16[32,64,512]{2,1,0:T(8,128)(2,1)} %select_select_fusion), calls=%async_computation | async-start | bytes 4194304 | tf_op jit(solution)/shard_map/all_to_all | solution.py:43
  123.3 78.4 %all-gather.5.cloned.1.call-done = f32[256,1024]{1,0:T(8,128)} async-done(((f32[8,1024]{1,0:T(8,128)}), f32[256,1024]{1,0:T(8,128)}) %all-gather.5.cloned.1.call-update) | async-done | bytes 1048592 | tf_op jit(solution)/shard_map/all_gather | solution.py:117
  201.6 1.0 slice_reduce_fusion
  202.7 0.7 iota_reduce_fusion
  203.9 2.1 slice.108
  206.0 2.3 gather_fusion.4
  208.3 0.9 copy.120
  209.2 0.8 copy.121
  210.0 1.0 broadcast_select_fusion.3
  210.9 0.8 log_add_fusion
  211.8 0.8 fusion.3
  212.5 1.0 copy-done
  213.5 0.8 fusion.5
  214.4 2.4 broadcast_in_dim.169
  216.9 2.5 scatter_fusion
  220.4 0.9 squeeze.45
  221.4 1.0 squeeze.44
  222.4 1.0 fusion.55
  224.0 46.7 %psum.14 = f32[1,4,191]{2,1,0:T(4,128)S(1)} all-reduce(f32[1,4,191]{2,1,0:T(4,128)S(1)} %bitcast.182), channel_id=1, replica_groups=mesh['grp'=4,'seq'=32,'mp'=4] {'seq'}, use_global_device_ids=true, to_apply=%region_13.14 | all-reduce | flops 764 | bytes 6112 | tf_op jit(solution)/shard_map/psum | solution.py:182
  270.7 9.6 %all_gather.15 = f32[4,4,191]{2,1,0:T(4,128)S(1)} all-gather(f32[1,4,191]{2,1,0:T(4,128)S(1)} %psum.14), channel_id=1, replica_groups=mesh['grp'=4,'seq'=32,'mp'=4] {'grp'}, dimensions={0}, use_global_device_ids=true | all-gather | bytes 15280 | tf_op jit(solution)/shard_map/all_gather | solution.py:183
  280.9 1.2 copy_select_fusion.1
  282.1 7.6 %psum.15 = f32[]{:T(128)} all-reduce(f32[]{:T(128)} %multiply_reduce_fusion.2), channel_id=1, replica_groups=mesh['grp'=4,'seq'=32,'mp'=4] {'mp'}, use_global_device_ids=true, to_apply=%region_16.17 | all-reduce | flops 1 | bytes 8 | tf_op jit(solution)/shard_map/psum | solution.py:185
  289.7 0.7 iota_reduce_fusion.2
  291.6 1.7 gather_fusion.1
  294.8 1.9 multiply_convert_fusion
  296.7 3.8 %copy.129 = bf16[1,8,128,2,512]{4,3,2,1,0:T(2,128)(2,1)} copy(bf16[1,8,128,2,512]{2,4,3,1,0:T(8,128)(2,1)S(1)} %bitcast.166) | data formatting | bytes 4194304
  301.3 2.2 gather_fusion.3
  304.4 6.6 %collective-permute-start = (bf16[64,512]{1,0:T(8,128)(2,1)S(1)}, bf16[64,512]{1,0:T(8,128)(2,1)S(1)}, u32[]{:S(2)}, u32[]{:S(2)}) collective-permute-start(bf16[64,512]{1,0:T(8,128)(2,1)S(1)} %bitcast.181), channel_id=1, source_target_pairs={{0,4},{4,8},{8,12},{12,16},{16,20},{20,24},{24,28},{28,32},{32,36}... | collective-permute-start | bytes 196616 | tf_op jit(solution)/shard_map/ppermute | solution.py:14
  311.2 1.8 collective-permute-done
  313.0 14.9 %reduce-scatter.2.cloned.1.call-done = bf16[1,2,64,512]{3,2,1,0:T(8,128)(2,1)} async-done(((bf16[32,2,64,512]{3,2,1,0:T(8,128)(2,1)}), bf16[1,2,64,512]{3,2,1,0:T(8,128)(2,1)}) %reduce-scatter.2.cloned.1.call-update) | async-done | bytes 131088 | tf_op jit(solution)/shard_map/reduce_scatter | solution.py:177
  327.9 0.8 slice_bitcast_fusion.1
  328.7 3.3 collective-permute-start.1
  332.8 0.9 slice.121
  334.2 0.7 maximum_bitcast_fusion.1
  (138 shorter events, 13.0 us)
Async XLA Ops:
  7.2 5.2 %copy-start.8 = (bf16[1,8,128,2,512]{4,3,2,1,0:T(2,128)(2,1)S(1)}, bf16[1,8,128,2,512]{4,3,2,1,0:T(2,128)(2,1)}, u32[]{:S(2)}) copy-start(bf16[1,8,128,2,512]{4,3,2,1,0:T(2,128)(2,1)} %param.8) | copy-start | bytes 6291460
  7.2 88.3 %all-gather.3.cloned.1.call-start = ((), (), s32[]{:S(2)}) async-start(), calls=%async_computation.2 | async-start | bytes 8650752 | tf_op jit(solution)/shard_map/all_gather | solution.py:61
  9.4 192.3 %all-gather.5.cloned.1.call-start = ((), (), s32[]{:S(2)}) async-start(), calls=%async_computation.3 | async-start | bytes 1081344 | tf_op jit(solution)/shard_map/all_gather | solution.py:117
  10.1 6.1 %copy-start.23 = (pred[8]{0:T(512)(128)(4,1)}, pred[8]{0:T(512)(128)(4,1)S(1)}, u32[]{:S(2)}) copy-start(pred[8]{0:T(512)(128)(4,1)S(1)} %get-tuple-element.54) | copy-start | bytes 28
  16.1 3.6 %copy-start.25 = (pred[64]{0:T(512)(128)(4,1)}, pred[64]{0:T(512)(128)(4,1)S(1)}, u32[]{:S(2)}) copy-start(pred[64]{0:T(512)(128)(4,1)S(1)} %iota_compare_fusion.2) | copy-start | bytes 196
  16.2 86.1 %copy-start.19 = (pred[8,64]{1,0:T(8,128)(4,1)}, pred[8,64]{1,0:T(8,128)(4,1)S(1)}, u32[]{:S(2)}) copy-start(pred[8,64]{1,0:T(8,128)(4,1)S(1)} %get-tuple-element.51) | copy-start | bytes 1540
  16.2 86.9 %copy-start.17 = (pred[8,64]{1,0:T(8,128)(4,1)}, pred[8,64]{1,0:T(8,128)(4,1)S(1)}, u32[]{:S(2)}) copy-start(pred[8,64]{1,0:T(8,128)(4,1)S(1)} %get-tuple-element.50) | copy-start | bytes 1540
  102.1 2.5 copy-start.4
  102.4 2.2 copy-start.2
  105.1 3.1 copy-start.24
  107.1 1.8 copy-start.14
  107.1 1.8 copy-start.15
  115.3 186.0 %all-to-all-start = ((bf16[32,64,512]{2,1,0:T(8,128)(2,1)}), bf16[32,64,512]{2,1,0:T(8,128)(2,1)}, u32[]{:S(2)}, u32[]{:S(2)}) async-start(bf16[32,64,512]{2,1,0:T(8,128)(2,1)} %select_select_fusion), calls=%async_computation | async-start | bytes 4194304 | tf_op jit(solution)/shard_map/all_to_all | solution.py:43
  123.2 88.6 %copy-start.9 = (bf16[8,64,4,128]{3,2,1,0:T(4,128)(2,1)S(1)}, bf16[8,64,4,128]{3,2,1,0:T(4,128)(2,1)}, u32[]{:S(2)}) copy-start(bf16[8,64,4,128]{3,2,1,0:T(4,128)(2,1)} %get-tuple-element.35) | copy-start | bytes 1572868
  123.2 204.7 %reduce-scatter.2.cloned.1.call-start = ((), (), s32[]{:S(2)}) async-start(), calls=%async_computation.4 | async-start | bytes 4325376 | tf_op jit(solution)/shard_map/reduce_scatter | solution.py:177
  202.7 3.3 copy-start.21
  210.0 3.5 %copy-start.3 = (bf16[8,128,1,512]{1,3,0,2:T(8,128)(2,1)S(1)}, bf16[8,128,1,512]{1,3,0,2:T(8,128)(2,1)}, u32[]{:S(2)}) copy-start(bf16[8,128,1,512]{1,3,0,2:T(8,128)(2,1)} %get-tuple-element.38) | copy-start | bytes 3145732
  211.7 2.6 copy-start.12
  212.5 1.0 copy-start
  214.4 2.4 copy-start.16
  219.4 0.7 copy-start.26
  219.4 1.0 copy-start.5
  219.4 3.0 copy-start.1
  221.4 59.5 %copy-start.6 = (bf16[8,1,64,4,128]{4,3,2,0,1:T(4,128)(2,1)S(1)}, bf16[8,1,64,4,128]{4,3,2,0,1:T(4,128)(2,1)}, u32[]{:S(2)}) copy-start(bf16[8,1,64,4,128]{4,3,2,0,1:T(4,128)(2,1)} %squeeze.45) | copy-start | bytes 1572868
  221.4 59.5 %copy-start.18 = (pred[8,64]{1,0:T(8,128)(4,1)S(1)}, pred[8,64]{1,0:T(8,128)(4,1)}, u32[]{:S(2)}) copy-start(pred[8,64]{1,0:T(8,128)(4,1)} %copy-done.17) | copy-start | bytes 1540
  221.4 59.5 %copy-start.20 = (pred[8,64]{1,0:T(8,128)(4,1)S(1)}, pred[8,64]{1,0:T(8,128)(4,1)}, u32[]{:S(2)}) copy-start(pred[8,64]{1,0:T(8,128)(4,1)} %copy-done.19) | copy-start | bytes 1540
  222.4 58.5 %copy-start.7 = (bf16[8,1,64,4,128]{4,3,2,0,1:T(4,128)(2,1)S(1)}, bf16[8,1,64,4,128]{4,3,2,0,1:T(4,128)(2,1)}, u32[]{:S(2)}) copy-start(bf16[8,1,64,4,128]{4,3,2,0,1:T(4,128)(2,1)} %squeeze.44) | copy-start | bytes 1572868
  223.4 66.4 %copy-start.22 = (f32[256]{0:T(256)S(1)}, f32[256]{0:T(256)}, u32[]{:S(2)}) copy-start(f32[256]{0:T(256)} %copy-done.21) | copy-start | bytes 3076
  223.5 71.0 %copy-start.13 = (f32[8,64,4]{1,2,0:T(4,128)S(1)}, f32[8,64,4]{1,2,0:T(4,128)}, u32[]{:S(2)}) copy-start(f32[8,64,4]{1,2,0:T(4,128)} %copy-done.12) | copy-start | bytes 24580
  282.1 12.7 %copy-start.10 = (bf16[8,1,64,4,128]{4,2,3,1,0:T(8,128)(2,1)S(1)}, bf16[8,1,64,4,128]{4,2,3,1,0:T(8,128)(2,1)}, u32[]{:S(2)}) copy-start(bf16[8,1,64,4,128]{4,2,3,1,0:T(8,128)(2,1)} %get-tuple-element.57) | copy-start | bytes 1572868
  282.1 12.7 %copy-start.11 = (bf16[8,1,64,4,128]{4,2,3,1,0:T(8,128)(2,1)S(1)}, bf16[8,1,64,4,128]{4,2,3,1,0:T(8,128)(2,1)}, u32[]{:S(2)}) copy-start(bf16[8,1,64,4,128]{4,2,3,1,0:T(8,128)(2,1)} %get-tuple-element.58) | copy-start | bytes 1572868
  296.7 3.8 %copy-start.28 = (pred[2,2]{1,0:T(4,128)(4,1)S(1)}, pred[2,2]{1,0:T(4,128)(4,1)}, u32[]{:S(2)}) copy-start(pred[2,2]{1,0:T(4,128)(4,1)} %broadcast_in_dim.155) | copy-start | bytes 16
  300.5 3.0 copy-start.27
  304.4 8.6 %collective-permute-start = (bf16[64,512]{1,0:T(8,128)(2,1)S(1)}, bf16[64,512]{1,0:T(8,128)(2,1)S(1)}, u32[]{:S(2)}, u32[]{:S(2)}) collective-permute-start(bf16[64,512]{1,0:T(8,128)(2,1)S(1)} %bitcast.181), channel_id=1, source_target_pairs={{0,4},{4,8},{8,12},{12,16},{16,20},{20,24},{24,28},{28,32},{32,36}... | collective-permute-start | bytes 196616 | tf_op jit(solution)/shard_map/ppermute | solution.py:14
  328.7 5.4 %collective-permute-start.1 = (bf16[64,512]{1,0:T(8,128)(2,1)S(1)}, bf16[64,512]{1,0:T(8,128)(2,1)S(1)}, u32[]{:S(2)}, u32[]{:S(2)}) collective-permute-start(bf16[64,512]{1,0:T(8,128)(2,1)S(1)} %slice_bitcast_fusion.1), channel_id=1, source_target_pairs={{0,4},{4,8},{8,12},{12,16},{16,20},{20,24},{24,28},{28,32},{32,36}... | collective-permute-start | bytes 196616 | tf_op jit(solution)/shard_map/ppermute | solution.py:14
Sparse Core Ops, SparseCore 0:
  10.1 85.2 all-gather.2
  108.3 93.3 all-gather.4
  219.5 108.3 reduce-scatter.1
